TPU v7x, 128 devices: a whole 4x4x4 slice. The times are simulated.
128 devices in a mesh: req: 16 (over y, z), mlp: 8 (over x, core).
Axes of the slice: x: 4, y: 4, z: 4, core: 2. Of those that a mesh axis runs over, the one named last changes fastest.
Arguments:
- resid: bfloat16 [2176, 5120], P('req', 'mlp'), may hold values from -180 to 180
- queries: bfloat16 [2176, 5120], P('req', 'mlp'), may hold values from -200 to 200
- new_keys: bfloat16 [2176, 1024], P('req', 'mlp'), may hold values from -6 to 6
- new_values: bfloat16 [2176, 1024], P('req', 'mlp'), may hold values from -6 to 6
- cache_keys: bfloat16 [48, 4096, 1024], P('req', None, 'mlp'), may hold values from -6 to 6
- cache_values: bfloat16 [48, 4096, 1024], P('req', None, 'mlp'), may hold values from -6 to 6
- context_keys: bfloat16 [5, 1024, 1024], P(None, 'req', 'mlp'), may hold values from -6 to 6
- context_values: bfloat16 [5, 1024, 1024], P(None, 'req', 'mlp'), may hold values from -6 to 6
- cache_lengths: int32 [48], P('req'), may hold values from 1 to 4096, 49152 in all
- group_ids: int32 [48], P('req'), may hold values from 0 to 3
- prefix_lengths: int32 [4], replicated, may hold values from 1 to 1024, 2048 in all
- prompt_start: int32 [1], replicated, may hold values from 1 to 1023
- out_weight: bfloat16 [5120, 5120], P('mlp'), may hold values from -1.25 to 1.25
- norm_gain: float32 [5120], P('mlp'), may hold values from 0.5 to 1.5
- gate_weight: bfloat16 [5120, 27648], P(None, ('req', 'mlp')), may hold values from -0.078125 to 0.078125
- up_weight: bfloat16 [5120, 27648], P(None, ('req', 'mlp')), may hold values from -0.078125 to 0.078125
- down_weight: bfloat16 [27648, 5120], P('req', 'mlp'), may hold values from -0.109375 to 0.109375
Outputs:
- out: bfloat16 [2176, 5120], P('req', 'mlp')
Inputs may be any that keep to these rules, and one draw needn't show every extreme that they name: `cache_lengths`: one decode request has 4096 valid positions. `prefix_lengths`: one group's prompt has 1024 positions.
All inputs are finite; a program needn't handle non-finite values. No bound on the sum of `cache_lengths` on one device may be relied on, other than what follows from the above.
Results may differ from a plain program's by a relative error of at most 0.019.
Values may be sent and summed in bfloat16 or wider, within the bound.
No kernel may reach another device: no remote copies, remote signals or barrier semaphores. Data moves between devices by JAX's collectives and lax.ppermute only.
A program may use at most 128 MiB of HBM per device.

v0:
```python
import math
import jax
import jax.numpy as jnp
from jax import lax
from jax.sharding import PartitionSpec as P

D = 5120
HQ = 40
KV = 8
HD = 128
NEGATIVE = -1e30


def absorb(carried, scores, allowed, values, pattern):
    running, totals, summed = carried
    scores = jnp.where(allowed, scores, -jnp.inf)
    highest = jnp.maximum(running, jnp.max(scores, axis=-1))
    exponent = jnp.where(allowed, jnp.exp(scores - highest[..., None]), 0.0)
    fading = jnp.exp(running - highest)
    weights = exponent.astype(jnp.bfloat16)
    summed = summed * fading[..., None] + jnp.einsum(
        pattern, weights, values, preferred_element_type=jnp.float32
    )
    totals = totals * fading + jnp.sum(exponent, axis=-1)
    return (highest, totals, summed)


def per_device(
    resid,
    queries,
    new_keys,
    new_values,
    cache_keys,
    cache_values,
    context_keys,
    context_values,
    cache_lengths,
    group_ids,
    prefix_lengths,
    prompt_start,
    out_weight,
    norm_gain,
    gate_weight,
    up_weight,
    down_weight,
):
    rows_here = queries.shape[0]
    decode_count = cache_keys.shape[0]
    prompt_count = rows_here - decode_count
    heads_kv = new_keys.shape[1] // HD
    group_size = HQ // KV
    scaling = 1.0 / math.sqrt(HD)
    cache_span = cache_keys.shape[1]
    context_count = context_keys.shape[0]
    query_rows = queries.reshape(rows_here, heads_kv, group_size, HD)
    query_decode = query_rows[:decode_count]
    query_prompt = query_rows[decode_count:]
    key_rows = new_keys.reshape(rows_here, heads_kv, HD)
    value_rows = new_values.reshape(rows_here, heads_kv, HD)

    def fresh_state(row_count):
        return (
            jnp.full((row_count, heads_kv, group_size), NEGATIVE, jnp.float32),
            jnp.zeros((row_count, heads_kv, group_size), jnp.float32),
            jnp.zeros((row_count, heads_kv, group_size, HD), jnp.float32),
        )

    past_keys = cache_keys.reshape(decode_count, cache_span, heads_kv, HD)
    past_values = cache_values.reshape(decode_count, cache_span, heads_kv, HD)
    scores = (
        jnp.einsum("ikgd,ickd->ikgc", query_decode, past_keys, preferred_element_type=jnp.float32)
        * scaling
    )
    usable = (jnp.arange(cache_span)[None, :] < cache_lengths[:, None])[:, None, None, :]
    decode_state = absorb(fresh_state(decode_count), scores, usable, past_values, "ikgc,ickd->ikgd")
    own_scores = (
        jnp.einsum(
            "ikgd,ikd->ikg",
            query_decode,
            key_rows[:decode_count],
            preferred_element_type=jnp.float32,
        )[..., None]
        * scaling
    )
    decode_state = absorb(
        decode_state,
        own_scores,
        jnp.ones(own_scores.shape, dtype=bool),
        value_rows[:decode_count][:, None],
        "ikgc,ickd->ikgd",
    )
    prompt_length = prompt_start[0]
    prefix_here = prefix_lengths[group_ids]
    state_decode = decode_state
    state_prompt = fresh_state(prompt_count)
    req_count = lax.axis_size("req")
    context_rows = context_keys.shape[1]
    context_pack = jnp.concatenate(
        [
            context_keys.reshape(context_count * context_rows, heads_kv * HD),
            context_values.reshape(context_count * context_rows, heads_kv * HD),
        ],
        0,
    )
    context_gathered = lax.all_gather(context_pack, "req", axis=0, tiled=False)
    new_pack = jnp.concatenate([new_keys, new_values], 0)
    new_copies = jnp.broadcast_to(new_pack[None], (req_count,) + new_pack.shape)
    new_gathered = lax.all_to_all(
        new_copies.reshape(req_count * new_pack.shape[0], -1), "req", 0, 0, tiled=True
    ).reshape(req_count, new_pack.shape[0], -1)
    context_span = context_count * context_rows

    def context_of(offset):
        piece = context_gathered[:, offset : offset + context_span]
        piece = piece.reshape(req_count, context_count, context_rows, heads_kv * HD)
        return jnp.transpose(piece, (1, 0, 2, 3)).reshape(
            context_count, req_count * context_rows, heads_kv * HD
        )

    def prompt_of(offset):
        piece = new_gathered[:, offset : offset + rows_here][:, decode_count:]
        return piece.reshape(req_count * prompt_count, heads_kv * HD)

    key_block = context_of(0)
    value_block = context_of(context_span)
    extent = key_block.shape[1]
    positions = jnp.arange(extent)
    key_split = key_block.reshape(context_count, extent, heads_kv, HD)
    value_split = value_block.reshape(context_count, extent, heads_kv, HD)
    chosen_keys = key_split[group_ids]
    chosen_values = value_split[group_ids]
    block_scores = (
        jnp.einsum("ikgd,ickd->ikgc", query_decode, chosen_keys, preferred_element_type=jnp.float32)
        * scaling
    )
    block_usable = (positions[None, :] < prefix_here[:, None])[:, None, None, :]
    state_decode = absorb(
        state_decode, block_scores, block_usable, chosen_values, "ikgc,ickd->ikgd"
    )
    block_scores = (
        jnp.einsum(
            "jkgd,ckd->jkgc",
            query_prompt,
            key_split[context_count - 1],
            preferred_element_type=jnp.float32,
        )
        * scaling
    )
    block_usable = (positions < prompt_length)[None, None, None, :]
    state_prompt = absorb(
        state_prompt, block_scores, block_usable, value_split[context_count - 1], "jkgc,ckd->jkgd"
    )
    prompt_state = state_prompt
    own_positions = lax.axis_index("req") * prompt_count + jnp.arange(prompt_count, dtype=jnp.int32)
    key_block = prompt_of(0)
    value_block = prompt_of(rows_here)
    extent = key_block.shape[0]
    positions = jnp.arange(extent, dtype=jnp.int32)
    block_scores = (
        jnp.einsum(
            "jkgd,ckd->jkgc",
            query_prompt,
            key_block.reshape(extent, heads_kv, HD),
            preferred_element_type=jnp.float32,
        )
        * scaling
    )
    block_usable = (positions[None, :] <= own_positions[:, None])[:, None, None, :]
    prompt_state = absorb(
        prompt_state,
        block_scores,
        block_usable,
        value_block.reshape(extent, heads_kv, HD),
        "jkgc,ckd->jkgd",
    )

    def finish(carried):
        return (carried[2] / carried[1][..., None]).astype(jnp.bfloat16)

    attended = jnp.concatenate([finish(state_decode), finish(prompt_state)], 0).reshape(
        rows_here, heads_kv * group_size * HD
    )
    mlp_count = lax.axis_size("mlp")
    head_partial = jnp.dot(attended, out_weight, preferred_element_type=jnp.float32)
    pieces = lax.all_to_all(head_partial.astype(jnp.bfloat16), "mlp", 1, 0, tiled=True)
    projected = jnp.sum(pieces.reshape(mlp_count, rows_here, -1).astype(jnp.float32), axis=0)
    mixed = (resid.astype(jnp.float32) + projected).astype(jnp.bfloat16)
    mixed_wide = mixed.astype(jnp.float32)
    mixed_rows = lax.all_gather(mixed, "mlp", axis=1, tiled=True).astype(jnp.float32)
    square_total = jnp.sum(mixed_rows * mixed_rows, axis=1)
    half = D // 2
    side = lax.axis_index("mlp") % 2
    own_half = lax.dynamic_slice_in_dim(mixed_rows, side * half, half, axis=1)
    own_gain = lax.dynamic_slice_in_dim(norm_gain, side * half, half, axis=0)
    normed = (own_half * lax.rsqrt(square_total / D + 1e-06)[:, None] * own_gain[None, :]).astype(
        jnp.bfloat16
    )
    near_rows = lax.all_gather(normed, "req", axis=0, tiled=True)
    pairs = [(i, i ^ 1) for i in range(mlp_count)]
    far_rows = lax.ppermute(near_rows, "mlp", pairs)

    def project(weight):
        near_weight = lax.dynamic_slice_in_dim(weight, side * half, half, axis=0)
        far_weight = lax.dynamic_slice_in_dim(weight, (1 - side) * half, half, axis=0)
        return jnp.dot(near_rows, near_weight, preferred_element_type=jnp.float32) + jnp.dot(
            far_rows, far_weight, preferred_element_type=jnp.float32
        )

    width = gate_weight.shape[1]
    both_proj = project(jnp.concatenate([gate_weight, up_weight], 1))
    gate_proj = both_proj[:, :width]
    up_proj = both_proj[:, width:]
    hidden = (jax.nn.silu(gate_proj) * up_proj).astype(jnp.bfloat16)
    hidden_block = lax.all_gather(hidden, "mlp", axis=1, tiled=True)
    down_partial = jnp.dot(hidden_block, down_weight, preferred_element_type=jnp.float32)
    req_pieces = lax.all_to_all(down_partial.astype(jnp.bfloat16), "req", 0, 0, tiled=True)
    feed = jnp.sum(req_pieces.reshape(req_count, rows_here, -1).astype(jnp.float32), axis=0)
    return (mixed_wide + feed).astype(jnp.bfloat16)


def solution(mesh):
    return jax.shard_map(
        per_device,
        mesh=mesh,
        in_specs=(
            P("req", "mlp"),
            P("req", "mlp"),
            P("req", "mlp"),
            P("req", "mlp"),
            P("req", None, "mlp"),
            P("req", None, "mlp"),
            P(None, "req", "mlp"),
            P(None, "req", "mlp"),
            P("req"),
            P("req"),
            P(),
            P(),
            P("mlp", None),
            P(),
            P(None, ("req", "mlp")),
            P(None, ("req", "mlp")),
            P("req", "mlp"),
        ),
        out_specs=P("req", "mlp"),
        check_vma=False,
    )
```

profile of v0, /device:TPU:0, one launch (start us, length us, event | category | flops | bytes accessed | tf_op | source)
XLA Modules:
  0.0 356.5 jit_solution(12019672314609117947)
XLA Ops:
  6.6 1.8 pad_maximum_fusion
  8.4 0.8 pad_maximum_fusion.1
  9.2 1.1 broadcast_in_dim.145
  10.3 8.2 %all-to-all-start = ((bf16[16,272,128]{2,1,0:T(8,128)(2,1)}), bf16[16,272,128]{2,1,0:T(8,128)(2,1)}, u32[]{:S(2)}, u32[]{:S(2)}) async-start(bf16[16,272,128]{2,1,0:T(8,128)(2,1)} %broadcast_in_dim.145), calls=%async_computation | async-start | bytes 2228224 | tf_op jit(solution)/shard_map/all_to_all | solution.py:108
  19.3 0.6 pad_clamp_fusion
  19.9 0.6 gather_fusion
  20.5 0.6 iota_compare_fusion.3
  21.1 0.7 slice_bitcast_fusion
  21.8 1.2 slice_convert_fusion
  23.0 0.7 iota_compare_fusion.2
  23.7 0.6 fusion.75
  24.4 0.5 iota_add_fusion
  25.0 0.9 reshape.390
  25.9 2.2 fusion.91
  28.2 0.2 iota_compare_fusion
  28.4 10.5 %all-to-all-done = bf16[16,272,128]{2,1,0:T(8,128)(2,1)} async-done(((bf16[16,272,128]{2,1,0:T(8,128)(2,1)}), bf16[16,272,128]{2,1,0:T(8,128)(2,1)}, u32[]{:S(2)}, u32[]{:S(2)}) %all-to-all-start) | async-done | bytes 1114144 | tf_op jit(solution)/shard_map/all_to_all | solution.py:108
  38.9 1.6 fusion.89
  40.5 1.0 reshape.439
  41.5 0.2 reshape.438
  41.7 3.7 %fusion.90 = (f32[133,5]{0,1:T(8,128)S(1)}, f32[133,1,5,2128]{3,0,2,1:T(8,128)}) fusion(bf16[2128,128,1]{1,0,2:T(8,128)(2,1)S(1)} %reshape.438, bf16[133,5,128]{2,1,0:T(8,128)(2,1)S(1)} %copy-done.5, pred[133,2128]{1,0:T(8,128)(4,1)S(1)} %iota_compare_fusion), kind=kOutput, calls=%fused_computation.124 | convolution fusion | flops 366515392 | bytes 6661172 | tf_op jit(solution)/shard_map/jkgd,ckd->jkgc/dot_general | solution.py:160
  45.4 18.5 %all-gather.14.cloned.1.call-done = bf16[10240,128]{1,0:T(8,128)(2,1)} async-done(((bf16[640,128]{1,0:T(8,128)(2,1)}), bf16[10240,128]{1,0:T(8,128)(2,1)}) %all-gather.14.cloned.1.call-update) | async-done | bytes 2621456 | tf_op jit(solution)/shard_map/all_gather | solution.py:105
  64.0 1.9 fusion.88
  65.9 0.7 slice.67
  66.6 1.3 copy.27
  67.9 0.7 slice.66
  68.6 1.2 copy.26
  69.8 2.1 gather_fusion.2
  71.9 3.0 gather_fusion.1
  75.0 1.6 fusion.92
  76.6 0.2 fusion.67
  76.8 0.3 fusion.69
  77.1 0.3 fusion.55
  77.3 0.9 multiply_add_fusion.1
  78.2 2.5 fusion.45
  80.7 0.7 bitcast_reduce_fusion
  81.5 1.4 fusion
  82.9 0.8 fusion.14
  83.8 0.8 fusion.34
  84.6 0.2 copy-done.9
  84.9 1.2 fusion.52
  86.3 0.9 slice-done.3
  87.1 1.3 convolution_convert_fusion
  88.6 23.8 %all_to_all.28 = bf16[136,8,640]{2,0,1:T(8,128)(2,1)S(1)} all-to-all(bf16[136,8,640]{2,0,1:T(8,128)(2,1)S(1)} %bitcast.174), channel_id=1, replica_groups=mesh['req'=16,'mlp'=8] {'mlp'}, dimensions={1} | all-to-all | bytes 2785280 | tf_op jit(solution)/shard_map/all_to_all | solution.py:185
  112.5 0.2 convert_reduce_fusion.1
  112.7 0.7 add_convert_fusion.1
  113.5 12.9 %all-gather.2 = f32[8,1,640]{2,1,0:T(1,128)S(1)} all-gather(f32[1,1,640]{2,1,0:T(1,128)S(1)} %reshape.432), channel_id=2, replica_groups=mesh['req'=16,'mlp'=8] {'mlp'}, dimensions={0}, use_global_device_ids=true | all-gather | bytes 23040 | tf_op args[13]
  126.5 8.4 %all-gather.8.cloned.1.call-done = bf16[136,5120]{1,0:T(8,128)(2,1)} async-done(((bf16[136,640]{1,0:T(8,128)(2,1)}), bf16[136,5120]{1,0:T(8,128)(2,1)}) %all-gather.8.cloned.1.call-update) | async-done | bytes 1392656 | tf_op jit(solution)/shard_map/all_gather | solution.py:189
  134.9 1.7 multiply_reduce_fusion
  136.6 1.8 convert_element_type.68
  138.4 1.1 multiply_convert_fusion
  139.6 83.5 %all-gather.10.cloned.1.call-done = bf16[2176,2560]{1,0:T(8,128)(2,1)} async-done(((bf16[136,2560]{1,0:T(8,128)(2,1)}), bf16[2176,2560]{1,0:T(8,128)(2,1)}) %all-gather.10.cloned.1.call-update) | async-done | bytes 11141136 | tf_op jit(solution)/shard_map/all_gather | solution.py:198
  223.0 0.1 constant_dynamic-update-slice_fusion.1
  223.2 1.5 copy-done.4
  224.7 0.1 constant_dynamic-update-slice_fusion
  224.8 8.4 %fusion.12 = f32[2176,432]{0,1:T(8,128)S(1)} fusion(bf16[2176,2560]{1,0:T(8,128)(2,1)} %all-gather.10.cloned.1.call-done, bf16[5120,432]{0,1:T(8,128)(2,1)S(1)} %constant_dynamic-update-slice_fusion, s32[]{:T(128)S(6)} %select_n.76), kind=kOutput, calls=%fused_computation.26 | convolution fusion | flops 4812963840 | bytes 17113092 | tf_op jit(solution)/shard_map/dot_general | solution.py:205
  233.2 7.2 %collective-permute-done = bf16[2176,2560]{1,0:T(8,128)(2,1)} collective-permute-done((bf16[2176,2560]{1,0:T(8,128)(2,1)}, bf16[2176,2560]{1,0:T(8,128)(2,1)}, u32[]{:S(2)}, u32[]{:S(2)}) %collective-permute-start) | collective-permute-done | bytes 11141152 | tf_op jit(solution)/shard_map/ppermute | solution.py:200
  240.5 8.5 %convolution_add_fusion = f32[2176,432]{0,1:T(8,128)S(1)} fusion(f32[2176,432]{0,1:T(8,128)S(1)} %fusion.12, bf16[2176,2560]{1,0:T(8,128)(2,1)} %collective-permute-done, bf16[5120,432]{0,1:T(8,128)(2,1)S(1)} %constant_dynamic-update-slice_fusion, s32[]{:T(128)S(6)} %select_n.77), kind=kOutput, calls=%fused_computation.10 | convolution fusion | flops 4813903872 | bytes 20873220 | tf_op jit(solution)/shard_map/dot_general | solution.py:205
  249.0 1.6 fusion.16
  250.6 45.7 %all-gather.12.cloned.1.call-done = bf16[2176,1728]{0,1:T(8,128)(2,1)} async-done(((bf16[2176,216]{0,1:T(8,128)(2,1)}), bf16[2176,1728]{0,1:T(8,128)(2,1)}) %all-gather.12.cloned.1.call-update) | async-done | bytes 7520272 | tf_op jit(solution)/shard_map/all_gather | solution.py:214
  296.3 9.0 %convolution_convert_fusion.1 = bf16[2176,640]{1,0:T(8,128)(2,1)S(1)} fusion(bf16[2176,1728]{0,1:T(8,128)(2,1)} %all-gather.12.cloned.1.call-done, bf16[1728,640]{1,0:T(8,128)(2,1)S(1)} %copy-done.23), kind=kOutput, calls=%fused_computation.9 | convolution fusion | flops 4814356480 | bytes 12517376 | tf_op jit(solution)/shard_map/dot_general | solution.py:215
  305.4 43.0 %all_to_all.29 = bf16[16,136,640]{2,1,0:T(8,128)(2,1)S(1)} all-to-all(bf16[16,136,640]{2,1,0:T(8,128)(2,1)S(1)} %bitcast.178), channel_id=1, replica_groups=mesh['req'=16,'mlp'=8] {'req'}, dimensions={0} | all-to-all | bytes 5570560 | tf_op jit(solution)/shard_map/all_to_all | solution.py:216
  348.4 0.4 convert_reduce_fusion
  348.8 0.5 copy-done.7
  349.3 0.7 add_convert_fusion
  (81 shorter events, 1.0 us)
Async XLA Ops:
  6.5 19.4 %copy-start = (bf16[3,4096,128]{2,1,0:T(8,128)(2,1)S(1)}, bf16[3,4096,128]{2,1,0:T(8,128)(2,1)}, u32[]{:S(2)}) copy-start(bf16[3,4096,128]{2,1,0:T(8,128)(2,1)} %param.21) | copy-start | bytes 9437188
  6.5 12.7 %copy-start.11 = (bf16[136,640]{1,0:T(8,128)(2,1)S(1)}, bf16[136,640]{1,0:T(8,128)(2,1)}, u32[]{:S(2)}) copy-start(bf16[136,640]{1,0:T(8,128)(2,1)} %param.18) | copy-start | bytes 522244
  6.5 12.7 %copy-start.24 = (s32[3]{0:T(128)S(1)}, s32[3]{0:T(128)}, u32[]{:S(2)}) copy-start(s32[3]{0:T(128)} %param.26) | copy-start | bytes 40
  6.5 13.3 %copy-start.2 = (s32[4]{0:T(128)S(1)}, s32[4]{0:T(128)}, u32[]{:S(2)}) copy-start(s32[4]{0:T(128)} %param.27) | copy-start | bytes 52
  6.5 17.8 %copy-start.22 = (s32[3]{0:T(128)S(1)}, s32[3]{0:T(128)}, u32[]{:S(2)}) copy-start(s32[3]{0:T(128)} %param.25) | copy-start | bytes 40
  6.5 57.4 %all-gather.14.cloned.1.call-start = ((), (), s32[]{:S(2)}) async-start(), calls=%async_computation.6 | async-start | bytes 2785280 | tf_op jit(solution)/shard_map/all_gather | solution.py:105
  10.3 28.6 %all-to-all-start = ((bf16[16,272,128]{2,1,0:T(8,128)(2,1)}), bf16[16,272,128]{2,1,0:T(8,128)(2,1)}, u32[]{:S(2)}, u32[]{:S(2)}) async-start(bf16[16,272,128]{2,1,0:T(8,128)(2,1)} %broadcast_in_dim.145), calls=%async_computation | async-start | bytes 2228224 | tf_op jit(solution)/shard_map/all_to_all | solution.py:108
  18.5 116.4 %all-gather.8.cloned.1.call-start = ((), (), s32[]{:S(2)}) async-start(), calls=%async_computation.3 | async-start | bytes 1566720 | tf_op jit(solution)/shard_map/all_gather | solution.py:189
  19.2 5.2 %copy-start.14 = (bf16[3,5,128]{2,1,0:T(8,128)(2,1)}, bf16[3,5,128]{2,1,0:T(8,128)(2,1)S(1)}, u32[]{:S(2)}) copy-start(bf16[3,5,128]{2,1,0:T(8,128)(2,1)S(1)} %reshape.382) | copy-start | bytes 11524
  25.9 2.2 copy-start.21
  28.2 13.6 %copy-start.5 = (bf16[133,5,128]{2,1,0:T(8,128)(2,1)S(1)}, bf16[133,5,128]{2,1,0:T(8,128)(2,1)}, u32[]{:S(2)}) copy-start(bf16[133,5,128]{2,1,0:T(8,128)(2,1)} %reshape.390) | copy-start | bytes 510724
  68.6 6.4 %copy-start.13 = (pred[3,1024]{1,0:T(4,128)(4,1)S(1)}, pred[3,1024]{1,0:T(4,128)(4,1)}, u32[]{:S(2)}) copy-start(pred[3,1024]{1,0:T(4,128)(4,1)} %iota_compare_fusion.2) | copy-start | bytes 9220
  68.6 6.4 %copy-start.15 = (bf16[3,5,128]{2,1,0:T(8,128)(2,1)S(1)}, bf16[3,5,128]{2,1,0:T(8,128)(2,1)}, u32[]{:S(2)}) copy-start(bf16[3,5,128]{2,1,0:T(8,128)(2,1)} %copy-done.14) | copy-start | bytes 11524
  68.6 8.0 %copy-start.16 = (f32[3,5]{1,0:T(4,128)S(1)}, f32[3,5]{1,0:T(4,128)}, u32[]{:S(2)}) copy-start(f32[3,5]{1,0:T(4,128)} %get-tuple-element.26) | copy-start | bytes 184
  68.6 8.0 %copy-start.19 = (f32[3,1,5]{2,1,0:T(1,128)S(1)}, f32[3,1,5]{2,1,0:T(1,128)}, u32[]{:S(2)}) copy-start(f32[3,1,5]{2,1,0:T(1,128)} %fusion.75) | copy-start | bytes 184
  68.6 12.8 %slice-start = ((s8[5918720]{0:T(1024)(128)(4,1)}), s8[1724416]{0:T(1024)(128)(4,1)S(1)}, s32[]{:S(2)}) async-start(s8[5918720]{0:T(1024)(128)(4,1)} %bitcast.166), calls=%async_computation.7 | async-start | bytes 3448832
  69.8 8.4 %copy-start.18 = (f32[3,128]{1,0:T(4,128)S(1)}, f32[3,128]{1,0:T(4,128)}, u32[]{:S(2)}) copy-start(f32[3,128]{1,0:T(4,128)} %slice_convert_fusion) | copy-start | bytes 4612
  75.0 5.7 %copy-start.6 = (bf16[133,5,128]{2,1,0:T(8,128)(2,1)S(1)}, bf16[133,5,128]{2,1,0:T(8,128)(2,1)}, u32[]{:S(2)}) copy-start(bf16[133,5,128]{2,1,0:T(8,128)(2,1)} %reshape.390) | copy-start | bytes 510724
  75.0 5.7 %copy-start.8 = (bf16[1,16,64,128]{3,2,0,1:T(8,128)(2,1)S(1)}, bf16[1,16,64,128]{3,2,0,1:T(8,128)(2,1)}, u32[]{:S(2)}) copy-start(bf16[1,16,64,128]{3,2,0,1:T(8,128)(2,1)} %slice.66) | copy-start | bytes 786436
  75.0 5.7 %copy-start.17 = (pred[1024]{0:T(1024)(128)(4,1)S(1)}, pred[1024]{0:T(1024)(128)(4,1)}, u32[]{:S(2)}) copy-start(pred[1024]{0:T(1024)(128)(4,1)} %iota_compare_fusion.3) | copy-start | bytes 3076
  76.8 4.7 %slice-start.1 = ((s8[5918720]{0:T(1024)(128)(4,1)}), s8[4194304]{0:T(1024)(128)(4,1)S(1)}, s32[]{:S(2)}) async-start(s8[5918720]{0:T(1024)(128)(4,1)} %bitcast.166), calls=%async_computation.8 | async-start | bytes 8388608
  82.9 1.0 copy-start.10
  83.8 1.0 copy-start.9
  83.8 2.5 slice-start.2
  84.9 2.3 slice-start.3
  88.6 24.1 %copy-start.12 = (bf16[136,640]{1,0:T(8,128)(2,1)S(1)}, bf16[136,640]{1,0:T(8,128)(2,1)}, u32[]{:S(2)}) copy-start(bf16[136,640]{1,0:T(8,128)(2,1)} %param.17) | copy-start | bytes 522244
  88.6 24.9 %copy-start.20 = (f32[640]{0:T(1024)S(1)}, f32[640]{0:T(1024)}, u32[]{:S(2)}) copy-start(f32[640]{0:T(1024)} %param.30) | copy-start | bytes 7684
  113.4 109.6 %all-gather.10.cloned.1.call-start = ((), (), s32[]{:S(2)}) async-start(), calls=%async_computation.4 | async-start | bytes 11837440 | tf_op jit(solution)/shard_map/all_gather | solution.py:198
  136.6 86.4 %copy-start.3 = (bf16[5120,216]{0,1:T(8,128)(2,1)S(1)}, bf16[5120,216]{0,1:T(8,128)(2,1)}, u32[]{:S(2)}) copy-start(bf16[5120,216]{0,1:T(8,128)(2,1)} %param.31) | copy-start | bytes 6635524
  139.5 156.8 %all-gather.12.cloned.1.call-start = ((), (), s32[]{:S(2)}) async-start(), calls=%async_computation.5 | async-start | bytes 8460288 | tf_op jit(solution)/shard_map/all_gather | solution.py:214
  223.0 17.4 %collective-permute-start = (bf16[2176,2560]{1,0:T(8,128)(2,1)}, bf16[2176,2560]{1,0:T(8,128)(2,1)}, u32[]{:S(2)}, u32[]{:S(2)}) collective-permute-start(bf16[2176,2560]{1,0:T(8,128)(2,1)} %all-gather.10.cloned.1.call-done), channel_id=1, source_target_pairs={{0,1},{1,0},{2,3},{3,2},{4,5},{5,4},{6,7},{7,6},{8,9},{9,8},{10,11... | collective-permute-start | bytes 33423368 | tf_op jit(solution)/shard_map/ppermute | solution.py:200
  223.0 1.6 copy-start.4
  249.0 47.3 %copy-start.23 = (bf16[1728,640]{1,0:T(8,128)(2,1)S(1)}, bf16[1728,640]{1,0:T(8,128)(2,1)}, u32[]{:S(2)}) copy-start(bf16[1728,640]{1,0:T(8,128)(2,1)} %param.33) | copy-start | bytes 6635524
  305.4 44.6 %copy-start.1 = (bf16[3,4096,128]{2,1,0:T(8,128)(2,1)S(1)}, bf16[3,4096,128]{2,1,0:T(8,128)(2,1)}, u32[]{:S(2)}) copy-start(bf16[3,4096,128]{2,1,0:T(8,128)(2,1)} %param.21) | copy-start | bytes 9437188
  348.4 0.9 copy-start.7
Sparse Core Ops, SparseCore 0:
  9.5 54.4 all-gather.13
  113.5 21.3 all-gather.7
  139.6 83.3 all-gather.9
  250.7 45.5 all-gather.11
where the time goes:
time: 357 us
  waiting for transfers between devices  174 us (49%)
  blocking collectives  79.7 us (22%)
  matrix products  40.9 us (11%)
  local copies, waits for them, and re-layouts  21.1 us (6%)
  other arithmetic  18.2 us (5%)
  between operations  14.2 us (4%)
  starting transfers between devices  8.37 us (2%)
    all_gather x1, waiting for transfers between devices, per_device(): near_rows = lax.all_gather(normed, 'req', axis=0, tiled=True)  83.5 us
    all_gather x1, waiting for transfers between devices, per_device(): hidden_block = lax.all_gather(hidden, 'mlp', axis=1, tiled=True)  45.7 us
    all_to_all x1, blocking collectives, per_device(): lax.all_to_all(down_partial.astype(jnp.bfloat16), 'req', 0, 0, tiled=True)  43 us
    all_to_all x1, blocking collectives, per_device(): lax.all_to_all(head_partial.astype(jnp.bfloat16), 'mlp', 1, 0, tiled=True)  23.8 us
    all_gather x1, waiting for transfers between devices, per_device(): context_gathered = lax.all_gather(context_pack, 'req', axis=0, tiled=False)  18.5 us
    unnamed x1, blocking collectives  12.9 us
    all_to_all x1, waiting for transfers between devices, per_device(): lax.all_to_all(new_copies.reshape(req_count * new_pack.shape[0], -1), 're...  10.5 us
    dot_general x1, matrix products, per_device(): jnp.dot(hidden_block, down_weight, preferred_element_type=jnp.float32)  9.03 us
  transfers between devices with their start and end apart: 6, of which 6 were waited for; matrix products, arithmetic and copies ran while one was open for 7% of the time, Pallas kernels for 0%

commit v1 on v0

--- a/solution.py
+++ b/solution.py
@@ -1,3 +1,4 @@
+import functools
 import math
 import jax
 import jax.numpy as jnp
@@ -9,6 +10,16 @@
 KV = 8
 HD = 128
 NEGATIVE = -1e30
+
+
+def _divide_racks(payload, link_axis):
+    taken_in = tuple((payload for _ in range(jax.lax.axis_size(link_axis))))
+    r2 = jax.lax.all_to_all(jnp.stack(taken_in), link_axis, 0, 0)
+    y2 = jnp.concatenate(r2, axis=0)
+    return y2
+
+
+_turn_classes = functools.partial(_divide_racks, link_axis="req")
 
 
 def absorb(carried, scores, allowed, values, pattern):
@@ -195,7 +206,7 @@
     normed = (own_half * lax.rsqrt(square_total / D + 1e-06)[:, None] * own_gain[None, :]).astype(
         jnp.bfloat16
     )
-    near_rows = lax.all_gather(normed, "req", axis=0, tiled=True)
+    near_rows = _turn_classes(normed)
     pairs = [(i, i ^ 1) for i in range(mlp_count)]
     far_rows = lax.ppermute(near_rows, "mlp", pairs)
 

time: 357 us -> 406 us (1.14)
  blocking collectives: 79.7 us -> 212 us
  waiting for transfers between devices: 174 us -> 87.6 us
    all_to_all x0 -> x1, blocking collectives: none -> 133 us  [_divide_racks(): r2 = jax.lax.all_to_all(jnp.stack(taken_in), link_axis, 0, 0)]
    all_gather x1 -> x0, waiting for transfers between devices: 83.5 us -> none  [per_device(): near_rows = lax.all_gather(normed, 'req', axis=0, tiled=True)]
    another operation x4 -> x5, local copies, waits for them, and re-layouts: 2.11 us -> 6.9 us  [the longest x1 4.79 us: _divide_racks(): r2 = jax.lax.all_to_all(jnp.stack(taken_in), link_axis, 0, 0)]
  transfers between devices with their start and end apart: 6 -> 5, of which waited for: 6 -> 5; matrix products, arithmetic and copies ran while one was open for 7% -> 6% of each run, Pallas kernels for 0% -> 0%
where the time goes in v1:
time: 406 us; the launch traced here: 405 us
  blocking collectives  212 us (52%)
  waiting for transfers between devices  87.6 us (22%)
  matrix products  39.9 us (10%)
  local copies, waits for them, and re-layouts  23.7 us (6%)
  other arithmetic  19.1 us (5%)
  between operations  14.3 us (4%)
  starting transfers between devices  8.33 us (2%)
    all_to_all x1, blocking collectives, _divide_racks(): r2 = jax.lax.all_to_all(jnp.stack(taken_in), link_axis, 0, 0)  133 us
    all_to_all x1, blocking collectives, per_device(): lax.all_to_all(down_partial.astype(jnp.bfloat16), 'req', 0, 0, tiled=True)  43 us
    all_gather x1, waiting for transfers between devices, per_device(): hidden_block = lax.all_gather(hidden, 'mlp', axis=1, tiled=True)  42.8 us
    all_to_all x1, blocking collectives, per_device(): lax.all_to_all(head_partial.astype(jnp.bfloat16), 'mlp', 1, 0, tiled=True)  23.8 us
    all_gather x1, waiting for transfers between devices, per_device(): context_gathered = lax.all_gather(context_pack, 'req', axis=0, tiled=False)  18.5 us
    unnamed x1, blocking collectives  12.9 us
    all_to_all x1, waiting for transfers between devices, per_device(): lax.all_to_all(new_copies.reshape(req_count * new_pack.shape[0], -1), 're...  10.5 us
    dot_general x1, matrix products, per_device(): jnp.dot(hidden_block, down_weight, preferred_element_type=jnp.float32)  9.03 us
  transfers between devices with their start and end apart: 5, of which 5 were waited for; matrix products, arithmetic and copies ran while one was open for 6% of the time, Pallas kernels for 0%

profile of v1, /device:TPU:0, one launch (start us, length us, event | category | flops | bytes accessed | tf_op | source)
XLA Modules:
  0.0 405.3 jit_solution(3939358673811223908)
XLA Ops:
  6.6 1.8 pad_maximum_fusion
  8.4 0.8 pad_maximum_fusion.1
  9.2 1.1 broadcast_in_dim.145
  10.3 8.2 %all-to-all-start = ((bf16[16,272,128]{2,1,0:T(8,128)(2,1)}), bf16[16,272,128]{2,1,0:T(8,128)(2,1)}, u32[]{:S(2)}, u32[]{:S(2)}) async-start(bf16[16,272,128]{2,1,0:T(8,128)(2,1)} %broadcast_in_dim.145), calls=%async_computation | async-start | bytes 2228224 | tf_op jit(solution)/shard_map/all_to_all | solution.py:119
  19.3 0.6 pad_clamp_fusion
  19.9 0.6 gather_fusion
  20.5 0.5 iota_compare_fusion.3
  21.1 0.7 slice_bitcast_fusion
  21.8 1.2 slice_convert_fusion
  23.0 0.7 iota_compare_fusion.2
  23.6 0.6 fusion.75
  24.4 0.6 iota_add_fusion
  25.0 0.9 reshape.395
  25.9 2.3 fusion.91
  28.2 0.2 iota_compare_fusion
  28.4 10.5 %all-to-all-done = bf16[16,272,128]{2,1,0:T(8,128)(2,1)} async-done(((bf16[16,272,128]{2,1,0:T(8,128)(2,1)}), bf16[16,272,128]{2,1,0:T(8,128)(2,1)}, u32[]{:S(2)}, u32[]{:S(2)}) %all-to-all-start) | async-done | bytes 1114144 | tf_op jit(solution)/shard_map/all_to_all | solution.py:119
  39.0 1.6 fusion.89
  40.5 1.0 reshape.445
  41.6 0.2 reshape.444
  41.7 3.7 fusion.90
  45.5 18.5 %all-gather.11.cloned.1.call-done = bf16[10240,128]{1,0:T(8,128)(2,1)} async-done(((bf16[640,128]{1,0:T(8,128)(2,1)}), bf16[10240,128]{1,0:T(8,128)(2,1)}) %all-gather.11.cloned.1.call-update) | async-done | bytes 2621456 | tf_op jit(solution)/shard_map/all_gather | solution.py:116
  64.0 1.9 fusion.88
  65.9 0.7 slice.67
  66.6 1.2 copy.27
  67.8 0.7 slice.66
  68.5 1.3 copy.26
  69.8 0.8 gather_fusion.2
  70.6 2.1 gather_fusion.1
  72.8 0.4 fusion.92
  73.2 0.2 fusion.67
  73.4 0.3 fusion.69
  73.7 0.3 fusion.55
  74.0 2.5 fusion.45
  76.5 0.7 bitcast_reduce_fusion
  77.2 4.2 %fusion = f32[133,5]{0,1:T(8,128)S(1)} fusion(f32[133,1,5,2128]{3,0,2,1:T(8,128)} %get-tuple-element.25, f32[133,5]{0,1:T(8,128)S(1)} %get-tuple-element.12, pred[133,2128]{1,0:T(8,128)(4,1)S(1)} %iota_compare_fusion), kind=kLoop, calls=%fused_computation.7 | loop fusion | flops 4244695 | bytes 5948824 | tf_op jit(solution)/shard_map/reduce_sum | solution.py:35
  81.4 0.8 fusion.14
  82.4 0.8 fusion.34
  83.2 0.5 slice-done.1
  83.8 1.4 fusion.52
  85.4 0.6 slice-done.3
  85.9 1.3 convolution_convert_fusion
  87.4 23.8 %all_to_all.33 = bf16[136,8,640]{2,0,1:T(8,128)(2,1)S(1)} all-to-all(bf16[136,8,640]{2,0,1:T(8,128)(2,1)S(1)} %bitcast.175), channel_id=1, replica_groups=mesh['req'=16,'mlp'=8] {'mlp'}, dimensions={1} | all-to-all | bytes 2785280 | tf_op jit(solution)/shard_map/all_to_all | solution.py:196
  111.3 0.2 convert_reduce_fusion.1
  111.5 0.7 add_convert_fusion.1
  112.3 12.9 %all-gather.2 = f32[8,1,640]{2,1,0:T(1,128)S(1)} all-gather(f32[1,1,640]{2,1,0:T(1,128)S(1)} %reshape.438), channel_id=2, replica_groups=mesh['req'=16,'mlp'=8] {'mlp'}, dimensions={0}, use_global_device_ids=true | all-gather | bytes 23040 | tf_op args[13]
  125.3 8.4 %all-gather.7.cloned.1.call-done = bf16[136,5120]{1,0:T(8,128)(2,1)} async-done(((bf16[136,640]{1,0:T(8,128)(2,1)}), bf16[136,5120]{1,0:T(8,128)(2,1)}) %all-gather.7.cloned.1.call-update) | async-done | bytes 1392656 | tf_op jit(solution)/shard_map/all_gather | solution.py:200
  133.7 1.7 multiply_reduce_fusion
  135.4 1.6 convert_element_type.68
  137.0 0.2 multiply_convert_fusion
  137.2 4.8 %stack.2 = bf16[16,136,2560]{2,1,0:T(8,128)(2,1)} broadcast(bf16[136,2560]{1,0:T(8,128)(2,1)S(1)} %multiply_convert_fusion), dimensions={1,2} | broadcast | bytes 11837440 | tf_op jit(solution)/shard_map/stack | solution.py:17
  142.0 132.7 %all_to_all.34 = bf16[16,136,2560]{2,1,0:T(8,128)(2,1)} all-to-all(bf16[16,136,2560]{2,1,0:T(8,128)(2,1)} %stack.2), channel_id=1, replica_groups=mesh['req'=16,'mlp'=8] {'req'}, dimensions={0} | all-to-all | bytes 22282240 | tf_op jit(solution)/shard_map/all_to_all | solution.py:17
  274.7 0.1 constant_dynamic-update-slice_fusion.1
  274.8 1.5 copy-done.5
  276.3 0.1 constant_dynamic-update-slice_fusion
  276.5 8.4 %fusion.12 = f32[2176,432]{0,1:T(8,128)S(1)} fusion(bf16[2176,2560]{1,0:T(8,128)(2,1)} %bitcast.29, bf16[5120,432]{0,1:T(8,128)(2,1)S(1)} %constant_dynamic-update-slice_fusion, s32[]{:T(128)S(6)} %select_n.76), kind=kOutput, calls=%fused_computation.26 | convolution fusion | flops 4812963840 | bytes 17113092 | tf_op jit(solution)/shard_map/dot_general | solution.py:216
  284.9 7.2 %collective-permute-done = bf16[2176,2560]{1,0:T(8,128)(2,1)} collective-permute-done((bf16[2176,2560]{1,0:T(8,128)(2,1)}, bf16[2176,2560]{1,0:T(8,128)(2,1)}, u32[]{:S(2)}, u32[]{:S(2)}) %collective-permute-start) | collective-permute-done | bytes 11141152 | tf_op jit(solution)/shard_map/ppermute | solution.py:211
  292.1 8.5 %convolution_add_fusion = f32[2176,432]{0,1:T(8,128)S(1)} fusion(f32[2176,432]{0,1:T(8,128)S(1)} %fusion.12, bf16[2176,2560]{1,0:T(8,128)(2,1)} %collective-permute-done, bf16[5120,432]{0,1:T(8,128)(2,1)S(1)} %constant_dynamic-update-slice_fusion, s32[]{:T(128)S(6)} %select_n.77), kind=kOutput, calls=%fused_computation.10 | convolution fusion | flops 4813903872 | bytes 20873220 | tf_op jit(solution)/shard_map/dot_general | solution.py:216
  300.6 1.6 fusion.16
  302.3 42.8 %all-gather.9.cloned.1.call-done = bf16[2176,1728]{0,1:T(8,128)(2,1)} async-done(((bf16[2176,216]{0,1:T(8,128)(2,1)}), bf16[2176,1728]{0,1:T(8,128)(2,1)}) %all-gather.9.cloned.1.call-update) | async-done | bytes 7520272 | tf_op jit(solution)/shard_map/all_gather | solution.py:225
  345.1 9.0 %convolution_convert_fusion.1 = bf16[2176,640]{1,0:T(8,128)(2,1)S(1)} fusion(bf16[2176,1728]{0,1:T(8,128)(2,1)} %all-gather.9.cloned.1.call-done, bf16[1728,640]{1,0:T(8,128)(2,1)S(1)} %copy-done.24), kind=kOutput, calls=%fused_computation.9 | convolution fusion | flops 4814356480 | bytes 12517376 | tf_op jit(solution)/shard_map/dot_general | solution.py:226
  354.1 43.0 %all_to_all.35 = bf16[16,136,640]{2,1,0:T(8,128)(2,1)S(1)} all-to-all(bf16[16,136,640]{2,1,0:T(8,128)(2,1)S(1)} %bitcast.179), channel_id=1, replica_groups=mesh['req'=16,'mlp'=8] {'req'}, dimensions={0} | all-to-all | bytes 5570560 | tf_op jit(solution)/shard_map/all_to_all | solution.py:227
  397.1 0.4 convert_reduce_fusion
  397.5 0.5 copy-done.8
  398.0 0.7 add_convert_fusion
  (82 shorter events, 1.1 us)
Async XLA Ops:
  6.5 19.3 %copy-start = (bf16[3,4096,128]{2,1,0:T(8,128)(2,1)S(1)}, bf16[3,4096,128]{2,1,0:T(8,128)(2,1)}, u32[]{:S(2)}) copy-start(bf16[3,4096,128]{2,1,0:T(8,128)(2,1)} %param.21) | copy-start | bytes 9437188
  6.5 12.7 %copy-start.12 = (bf16[136,640]{1,0:T(8,128)(2,1)S(1)}, bf16[136,640]{1,0:T(8,128)(2,1)}, u32[]{:S(2)}) copy-start(bf16[136,640]{1,0:T(8,128)(2,1)} %param.18) | copy-start | bytes 522244
  6.5 12.7 %copy-start.25 = (s32[3]{0:T(128)S(1)}, s32[3]{0:T(128)}, u32[]{:S(2)}) copy-start(s32[3]{0:T(128)} %param.26) | copy-start | bytes 40
  6.5 13.3 %copy-start.2 = (s32[4]{0:T(128)S(1)}, s32[4]{0:T(128)}, u32[]{:S(2)}) copy-start(s32[4]{0:T(128)} %param.27) | copy-start | bytes 52
  6.5 17.7 %copy-start.23 = (s32[3]{0:T(128)S(1)}, s32[3]{0:T(128)}, u32[]{:S(2)}) copy-start(s32[3]{0:T(128)} %param.25) | copy-start | bytes 40
  6.5 57.4 %all-gather.11.cloned.1.call-start = ((), (), s32[]{:S(2)}) async-start(), calls=%async_computation.6 | async-start | bytes 2785280 | tf_op jit(solution)/shard_map/all_gather | solution.py:116
  10.3 28.6 %all-to-all-start = ((bf16[16,272,128]{2,1,0:T(8,128)(2,1)}), bf16[16,272,128]{2,1,0:T(8,128)(2,1)}, u32[]{:S(2)}, u32[]{:S(2)}) async-start(bf16[16,272,128]{2,1,0:T(8,128)(2,1)} %broadcast_in_dim.145), calls=%async_computation | async-start | bytes 2228224 | tf_op jit(solution)/shard_map/all_to_all | solution.py:119
  18.5 115.2 %all-gather.7.cloned.1.call-start = ((), (), s32[]{:S(2)}) async-start(), calls=%async_computation.4 | async-start | bytes 1566720 | tf_op jit(solution)/shard_map/all_gather | solution.py:200
  19.3 5.1 %copy-start.15 = (bf16[3,5,128]{2,1,0:T(8,128)(2,1)}, bf16[3,5,128]{2,1,0:T(8,128)(2,1)S(1)}, u32[]{:S(2)}) copy-start(bf16[3,5,128]{2,1,0:T(8,128)(2,1)S(1)} %reshape.387) | copy-start | bytes 11524
  25.9 2.3 copy-start.22
  28.2 13.6 %copy-start.6 = (bf16[133,5,128]{2,1,0:T(8,128)(2,1)S(1)}, bf16[133,5,128]{2,1,0:T(8,128)(2,1)}, u32[]{:S(2)}) copy-start(bf16[133,5,128]{2,1,0:T(8,128)(2,1)} %reshape.395) | copy-start | bytes 510724
  67.8 2.0 copy-start.3
  68.5 4.3 %copy-start.14 = (pred[3,1024]{1,0:T(4,128)(4,1)S(1)}, pred[3,1024]{1,0:T(4,128)(4,1)}, u32[]{:S(2)}) copy-start(pred[3,1024]{1,0:T(4,128)(4,1)} %iota_compare_fusion.2) | copy-start | bytes 9220
  68.5 4.3 %copy-start.16 = (bf16[3,5,128]{2,1,0:T(8,128)(2,1)S(1)}, bf16[3,5,128]{2,1,0:T(8,128)(2,1)}, u32[]{:S(2)}) copy-start(bf16[3,5,128]{2,1,0:T(8,128)(2,1)} %copy-done.15) | copy-start | bytes 11524
  68.5 4.7 %copy-start.17 = (f32[3,5]{1,0:T(4,128)S(1)}, f32[3,5]{1,0:T(4,128)}, u32[]{:S(2)}) copy-start(f32[3,5]{1,0:T(4,128)} %get-tuple-element.26) | copy-start | bytes 184
  68.5 4.7 %copy-start.20 = (f32[3,1,5]{2,1,0:T(1,128)S(1)}, f32[3,1,5]{2,1,0:T(1,128)}, u32[]{:S(2)}) copy-start(f32[3,1,5]{2,1,0:T(1,128)} %fusion.75) | copy-start | bytes 184
  69.8 4.2 %copy-start.19 = (f32[3,128]{1,0:T(4,128)S(1)}, f32[3,128]{1,0:T(4,128)}, u32[]{:S(2)}) copy-start(f32[3,128]{1,0:T(4,128)} %slice_convert_fusion) | copy-start | bytes 4612
  72.8 3.7 copy-start.7
  72.8 3.7 copy-start.9
  72.8 3.7 copy-start.18
  77.2 6.0 %slice-start = ((s8[5918720]{0:T(1024)(128)(4,1)}), s8[1724416]{0:T(1024)(128)(4,1)S(1)}, s32[]{:S(2)}) async-start(s8[5918720]{0:T(1024)(128)(4,1)} %bitcast.167), calls=%async_computation.7 | async-start | bytes 3448832
  81.4 1.0 copy-start.11
  81.4 2.3 slice-start.1
  81.4 2.4 copy-start.10
  82.4 3.0 slice-start.2
  83.8 2.1 slice-start.3
  87.4 24.1 %copy-start.13 = (bf16[136,640]{1,0:T(8,128)(2,1)S(1)}, bf16[136,640]{1,0:T(8,128)(2,1)}, u32[]{:S(2)}) copy-start(bf16[136,640]{1,0:T(8,128)(2,1)} %param.17) | copy-start | bytes 522244
  87.4 24.8 %copy-start.21 = (f32[640]{0:T(1024)S(1)}, f32[640]{0:T(1024)}, u32[]{:S(2)}) copy-start(f32[640]{0:T(1024)} %param.30) | copy-start | bytes 7684
  112.2 232.9 %all-gather.9.cloned.1.call-start = ((), (), s32[]{:S(2)}) async-start(), calls=%async_computation.5 | async-start | bytes 8460288 | tf_op jit(solution)/shard_map/all_gather | solution.py:225
  142.0 132.7 %copy-start.4 = (bf16[5120,216]{0,1:T(8,128)(2,1)S(1)}, bf16[5120,216]{0,1:T(8,128)(2,1)}, u32[]{:S(2)}) copy-start(bf16[5120,216]{0,1:T(8,128)(2,1)} %param.31) | copy-start | bytes 6635524
  274.7 17.4 %collective-permute-start = (bf16[2176,2560]{1,0:T(8,128)(2,1)}, bf16[2176,2560]{1,0:T(8,128)(2,1)}, u32[]{:S(2)}, u32[]{:S(2)}) collective-permute-start(bf16[2176,2560]{1,0:T(8,128)(2,1)} %bitcast.29), channel_id=1, source_target_pairs={{0,1},{1,0},{2,3},{3,2},{4,5},{5,4},{6,7},{7,6},{8,9},{9,8},{10,11... | collective-permute-start | bytes 33423368 | tf_op jit(solution)/shard_map/ppermute | solution.py:211
  274.7 1.6 copy-start.5
  300.6 44.5 %copy-start.24 = (bf16[1728,640]{1,0:T(8,128)(2,1)S(1)}, bf16[1728,640]{1,0:T(8,128)(2,1)}, u32[]{:S(2)}) copy-start(bf16[1728,640]{1,0:T(8,128)(2,1)} %param.33) | copy-start | bytes 6635524
  354.1 44.6 %copy-start.1 = (bf16[3,4096,128]{2,1,0:T(8,128)(2,1)S(1)}, bf16[3,4096,128]{2,1,0:T(8,128)(2,1)}, u32[]{:S(2)}) copy-start(bf16[3,4096,128]{2,1,0:T(8,128)(2,1)} %param.21) | copy-start | bytes 9437188
  397.1 0.9 copy-start.8
Sparse Core Ops, SparseCore 0:
  9.5 54.4 all-gather.10
  112.3 21.3 all-gather.6
  302.4 42.6 all-gather.8
